TPU v7x, 256 devices: a whole 4x4x8 slice. The times are simulated.
256 devices in a mesh: group: 4 (over y), shard: 16 (over x_hi, z), tensor: 4 (over x_lo, core).
Axes of the slice: x: 4 (x_hi: 2, x_lo: 2; x = x_hi * 2 + x_lo), y: 4, z: 8, core: 2. Of those that a mesh axis runs over, the one named last changes fastest.
Arguments:
- group_weights: bfloat16 [4, 8, 1024, 8704], P('group', None, None, ('shard', 'tensor')), may hold values from -6 to 6
- anchor: float32 [8, 1024, 16, 4, 136], P(None, ('group', 'shard'), None, 'tensor'), may hold values from -6 to 6
- momentum: float32 [8, 1024, 16, 4, 136], P(None, ('group', 'shard'), None, 'tensor'), may hold values from -6 to 6
- group_embedding: bfloat16 [4, 32000, 1024], P('group', 'shard', 'tensor'), may hold values from -6 to 6
- emb_anchor: float32 [32000, 1024], P('shard', 'tensor'), may hold values from -6 to 6
- emb_momentum: float32 [32000, 1024], P('shard', 'tensor'), may hold values from -6 to 6
- basis: float32 [1024, 64], P('tensor'), may hold values from -0.1875 to 0.1875
Outputs:
- new_weights: bfloat16 [8, 1024, 8704], P(None, None, ('shard', 'tensor'))
- new_anchor: float32 [8, 1024, 16, 4, 136], P(None, ('group', 'shard'), None, 'tensor')
- new_momentum: float32 [8, 1024, 16, 4, 136], P(None, ('group', 'shard'), None, 'tensor')
- new_embedding: bfloat16 [32000, 1024], P('shard', 'tensor')
- new_emb_anchor: float32 [32000, 1024], P('shard', 'tensor')
- new_emb_momentum: float32 [32000, 1024], P('shard', 'tensor')
All inputs are finite; a program needn't handle non-finite values.
Results may differ from a plain program's by a relative error of at most 0.012.
Values may be sent and summed in bfloat16 or wider, within the bound.
No kernel may reach another device: no remote copies, remote signals or barrier semaphores. Data moves between devices by JAX's collectives and lax.ppermute only.
A program may use at most 128 MiB of HBM per device.

v0:
```python
import jax
import jax.numpy as jnp
from jax import lax
from jax.sharding import PartitionSpec as P

outer_rate = 0.7
momentum_decay = 0.9


def per_device(group_weights, anchor, momentum, group_embedding, emb_anchor, emb_momentum, basis):
    groups = lax.axis_size("group")
    layers = group_weights.shape[1]
    width = group_weights.shape[2]
    block = group_weights.shape[3]
    local_weights = group_weights[0]
    part = lax.psum_scatter(
        local_weights.astype(jnp.float32).astype(jnp.bfloat16),
        "group",
        scatter_dimension=1,
        tiled=True,
    ).astype(jnp.float32)
    part = part.reshape(layers, part.shape[1], 1, 1, block)
    summed = lax.all_to_all(part, "shard", split_axis=1, concat_axis=2, tiled=True)
    delta = anchor - summed / groups
    moved = momentum_decay * momentum + delta
    stepped = anchor - outer_rate * (delta + momentum_decay * moved)
    stepped_half = stepped.astype(jnp.bfloat16)
    columns = lax.all_to_all(stepped_half, "shard", split_axis=2, concat_axis=1, tiled=True)
    whole = lax.all_gather(columns, "group", axis=1, tiled=True)
    new_weights = whole.reshape(layers, width, block)
    local_embedding = group_embedding[0].astype(jnp.float32)
    emb_sum = lax.psum(local_embedding.astype(jnp.bfloat16), "group").astype(jnp.float32)
    difference = emb_anchor - emb_sum / groups
    coef = lax.psum(jnp.dot(difference, basis, precision=lax.Precision.HIGHEST), "tensor")
    emb_delta = jnp.dot(coef, basis.T, precision=lax.Precision.HIGHEST)
    emb_moved = momentum_decay * emb_momentum + emb_delta
    emb_stepped = emb_anchor - outer_rate * (emb_delta + momentum_decay * emb_moved)
    return (new_weights, stepped, moved, emb_stepped.astype(jnp.bfloat16), emb_stepped, emb_moved)


def solution(mesh):
    return jax.shard_map(
        per_device,
        mesh=mesh,
        in_specs=(
            P("group", None, None, ("shard", "tensor")),
            P(None, ("group", "shard"), None, "tensor", None),
            P(None, ("group", "shard"), None, "tensor", None),
            P("group", "shard", "tensor"),
            P("shard", "tensor"),
            P("shard", "tensor"),
            P("tensor", None),
        ),
        out_specs=(
            P(None, None, ("shard", "tensor")),
            P(None, ("group", "shard"), None, "tensor", None),
            P(None, ("group", "shard"), None, "tensor", None),
            P("shard", "tensor"),
            P("shard", "tensor"),
            P("shard", "tensor"),
        ),
        check_vma=False,
    )
```

profile of v0, /device:TPU:1, one launch (start us, length us, event | category | flops | bytes accessed | tf_op | source)
XLA Modules:
  0.0 260.1 jit_solution(16609563485341192564)
XLA Ops:
  7.2 0.0 copy-start
  7.2 0.0 reduce-scatter.2.cloned.1.call-start
  7.2 6.8 %copy.20 = bf16[1,8,1024,136]{3,1,2,0:T(8,128)(2,1)} copy(bf16[1,8,1024,136]{2,3,1,0:T(8,128)(2,1)} %param.7) | data formatting | bytes 4456448 | tf_op args[0]
  14.0 0.0 reduce-scatter.2.cloned.1.call-update
  14.0 53.3 %reduce-scatter.2.cloned.1.call-done = bf16[8,256,136]{2,0,1:T(8,128)(2,1)} async-done(((bf16[8,1024,136]{2,0,1:T(8,128)(2,1)}), bf16[8,256,136]{2,0,1:T(8,128)(2,1)}) %reduce-scatter.2.cloned.1.call-update) | async-done | bytes 557072 | tf_op jit(solution)/shard_map/reduce_scatter | solution.py:16
  67.3 2.7 %bitcast_convert_fusion = f32[8,256,1,1,136]{4,0,3,2,1:T(8,128)} fusion(bf16[8,256,136]{2,0,1:T(8,128)(2,1)} %reduce-scatter.2.cloned.1.call-done), kind=kLoop, calls=%fused_computation.11 | loop fusion | flops 278528 | bytes 1671168 | tf_op jit(solution)/shard_map/reshape | solution.py:22
  70.0 9.2 %all-to-all-start = ((f32[8,256,1,1,136]{4,0,3,2,1:T(8,128)}), f32[8,256,1,1,136]{4,0,3,2,1:T(8,128)S(1)}, u32[]{:S(2)}, u32[]{:S(2)}) async-start(f32[8,256,1,1,136]{4,0,3,2,1:T(8,128)} %bitcast_convert_fusion), calls=%async_computation.1 | async-start | bytes 4194304 | tf_op jit(solution)/shard_map/all_to_all | solution.py:23
  79.3 0.0 all-reduce.3.cloned.1.call-start
  79.3 0.7 all-reduce.3.cloned.1.call-update
  80.0 48.4 %all-to-all-done = f32[8,256,1,1,136]{4,0,3,2,1:T(8,128)S(1)} async-done(((f32[8,256,1,1,136]{4,0,3,2,1:T(8,128)}), f32[8,256,1,1,136]{4,0,3,2,1:T(8,128)S(1)}, u32[]{:S(2)}, u32[]{:S(2)}) %all-to-all-start) | async-done | bytes 1114144 | tf_op jit(solution)/shard_map/all_to_all | solution.py:23
  128.5 0.7 copy_multiply_fusion.1
  129.2 0.9 copy-done.2
  130.1 0.6 copy-done.3
  130.7 5.1 %fusion.8 = (bf16[8,16,16,1,136]{4,1,2,0,3:T(8,128)(2,1)S(1)}, f32[8,16,16,1,136]{4,1,2,0,3:T(8,128)}, f32[8,16,16,1,136]{4,1,2,0,3:T(8,128)S(1)}) fusion(f32[8,16,16,1,136]{4,3,2,1,0:T(1,128)S(1)} %copy-done.2, f32[8,16,16,1,136]{4,1,2,0,3:T(8,128)S(1)} %bitcast.19, f32[8,16,16,1,136]{4,3,2,1,0:T(1,128)S(1)} %copy-done.3), kind=kLoop, calls=%fused_computation.15 | loop fusion | flops 2228224 | bytes 6127616 | tf_op jit(solution)/shard_map/convert_element_type | solution.py:27
  135.8 1.1 copy.25
  136.9 7.1 %all-to-all-start.1 = ((bf16[8,16,16,1,136]{4,1,0,3,2:T(8,128)(2,1)}), bf16[8,16,16,1,136]{4,1,0,3,2:T(8,128)(2,1)S(1)}, u32[]{:S(2)}, u32[]{:S(2)}) async-start(bf16[8,16,16,1,136]{4,1,0,3,2:T(8,128)(2,1)} %copy.25), calls=%async_computation.2 | async-start | bytes 2097152 | tf_op jit(solution)/shard_map/all_to_all | solution.py:28
  144.0 0.0 all-reduce.5.cloned.1.call-start
  144.1 0.0 all-reduce.3.cloned.1.call-done
  144.1 0.0 copy-done
  144.1 4.8 %fusion.1 = f32[2000,64]{0,1:T(8,128)} fusion(f32[256,64]{0,1:T(8,128)S(1)} %copy-done, f32[2000,256]{1,0:T(8,128)} %param.11, bf16[2000,256]{1,0:T(8,128)(2,1)} %all-reduce.3.cloned.1.call-done), kind=kOutput, calls=%fused_computation.6 | convolution fusion | flops 394752000 | bytes 3649536 | tf_op jit(solution)/shard_map/dot_general | solution.py:34
  148.9 0.0 all-reduce.5.cloned.1.call-update
  148.9 0.2 all-gather.2.cloned.1.call-start
  149.1 21.9 %all-to-all-done.1 = bf16[8,16,16,1,136]{4,1,0,3,2:T(8,128)(2,1)S(1)} async-done(((bf16[8,16,16,1,136]{4,1,0,3,2:T(8,128)(2,1)}), bf16[8,16,16,1,136]{4,1,0,3,2:T(8,128)(2,1)S(1)}, u32[]{:S(2)}, u32[]{:S(2)}) %all-to-all-start.1) | async-done | bytes 557088 | tf_op jit(solution)/shard_map/all_to_all | solution.py:28
  171.1 1.1 copy.26
  172.2 0.0 all-gather.2.cloned.1.call-update
  172.2 22.1 %all-reduce.5.cloned.1.call-done = f32[2000,64]{0,1:T(8,128)} async-done(((f32[2000,64]{0,1:T(8,128)}), f32[2000,64]{0,1:T(8,128)}) %all-reduce.5.cloned.1.call-update) | async-done | bytes 512016 | tf_op jit(solution)/shard_map/psum | solution.py:34
  194.3 6.9 %fusion.7 = (bf16[2000,256]{1,0:T(8,128)(2,1)}, f32[2000,256]{1,0:T(8,128)}, f32[2000,256]{1,0:T(8,128)}) fusion(f32[2000,256]{1,0:T(8,128)} %param.11, f32[2000,256]{1,0:T(8,128)} %param.12, f32[2000,64]{0,1:T(8,128)} %all-reduce.5.cloned.1.call-done, f32[256,64]{0,1:T(8,128)S(1)} %copy-done), kind=kOutput, calls=%fused_computation.14 | convolution fusion | flops 396800000 | bytes 9793536 | tf_op jit(solution)/shard_map/dot_general | solution.py:35
  201.3 0.0 copy-done.1
  201.3 3.7 %copy.28 = f32[8,16,16,1,136]{4,3,2,1,0:T(1,128)} copy(f32[8,16,16,1,136]{4,1,2,0,3:T(8,128)S(1)} %copy-done.1) | data formatting | bytes 2228224
  205.0 3.7 %copy.29 = f32[8,16,16,1,136]{4,3,2,1,0:T(1,128)} copy(f32[8,16,16,1,136]{4,1,2,0,3:T(8,128)S(1)} %get-tuple-element.23) | data formatting | bytes 2228224
  208.7 39.0 %all-gather.2.cloned.1.call-done = bf16[8,1024,1,1,136]{4,1,0,3,2:T(8,128)(2,1)} async-done(((bf16[8,256,1,1,136]{4,1,0,3,2:T(8,128)(2,1)}), bf16[8,1024,1,1,136]{4,1,0,3,2:T(8,128)(2,1)}) %all-gather.2.cloned.1.call-update) | async-done | bytes 2228240 | tf_op jit(solution)/shard_map/all_gather | solution.py:29
  247.7 5.9 %copy.27 = bf16[8,1024,136]{1,2,0:T(8,128)(2,1)} copy(bf16[8,1024,136]{2,1,0:T(8,128)(2,1)} %bitcast.20) | data formatting | bytes 4456448
  (3 shorter events, 0.0 us)
Async XLA Ops:
  7.2 136.9 %copy-start = (f32[256,64]{0,1:T(8,128)S(1)}, f32[256,64]{0,1:T(8,128)}, u32[]{:S(2)}) copy-start(f32[256,64]{0,1:T(8,128)} %param.13) | copy-start | bytes 196612
  7.2 60.1 %reduce-scatter.2.cloned.1.call-start = ((), (), s32[]{:S(2)}) async-start(), calls=%async_computation.3 | async-start | bytes 5242880 | tf_op jit(solution)/shard_map/reduce_scatter | solution.py:16
  70.0 58.4 %all-to-all-start = ((f32[8,256,1,1,136]{4,0,3,2,1:T(8,128)}), f32[8,256,1,1,136]{4,0,3,2,1:T(8,128)S(1)}, u32[]{:S(2)}, u32[]{:S(2)}) async-start(f32[8,256,1,1,136]{4,0,3,2,1:T(8,128)} %bitcast_convert_fusion), calls=%async_computation.1 | async-start | bytes 4194304 | tf_op jit(solution)/shard_map/all_to_all | solution.py:23
  79.3 64.8 %all-reduce.3.cloned.1.call-start = ((), (), s32[]{:S(2)}) async-start(), calls=%async_computation.5 | async-start | bytes 2048000 | tf_op jit(solution)/shard_map/psum | solution.py:32
  128.5 1.6 copy-start.2
  128.5 2.3 copy-start.3
  136.9 34.2 %all-to-all-start.1 = ((bf16[8,16,16,1,136]{4,1,0,3,2:T(8,128)(2,1)}), bf16[8,16,16,1,136]{4,1,0,3,2:T(8,128)(2,1)S(1)}, u32[]{:S(2)}, u32[]{:S(2)}) async-start(bf16[8,16,16,1,136]{4,1,0,3,2:T(8,128)(2,1)} %copy.25), calls=%async_computation.2 | async-start | bytes 2097152 | tf_op jit(solution)/shard_map/all_to_all | solution.py:28
  144.0 50.3 %all-reduce.5.cloned.1.call-start = ((), (), s32[]{:S(2)}) async-start(), calls=%async_computation.6 | async-start | bytes 1048576 | tf_op jit(solution)/shard_map/psum | solution.py:34
  148.9 98.8 %all-gather.2.cloned.1.call-start = ((), (), s32[]{:S(2)}) async-start(), calls=%async_computation.4 | async-start | bytes 5242880 | tf_op jit(solution)/shard_map/all_gather | solution.py:29
  194.3 6.9 %copy-start.1 = (f32[8,16,16,1,136]{4,1,2,0,3:T(8,128)S(1)}, f32[8,16,16,1,136]{4,1,2,0,3:T(8,128)}, u32[]{:S(2)}) copy-start(f32[8,16,16,1,136]{4,1,2,0,3:T(8,128)} %get-tuple-element.22) | copy-start | bytes 3342340
Sparse Core Ops, SparseCore 0:
  14.1 53.1 reduce-scatter.1
  82.4 50.1 all-reduce.2
  149.0 45.2 all-reduce.4
  196.6 51.0 all-gather.1
where the time goes:
time: 261 us; the launch traced here: 260 us
  waiting for transfers between devices  186 us (71%)
  local copies, waits for them, and re-layouts  23.8 us (9%)
  starting transfers between devices  16.7 us (6%)
  between operations  13.8 us (5%)
  matrix products  11.7 us (4%)
  other arithmetic  8.55 us (3%)
    reduce_scatter x1, waiting for transfers between devices, per_device(): lax.psum_scatter(local_weights.astype(jnp.float32).astype(jnp.bfloat16),...  53.3 us
    all_to_all x1, waiting for transfers between devices, per_device(): lax.all_to_all(part, 'shard', split_axis=1, concat_axis=2, tiled=True)  48.4 us
    all_gather x1, waiting for transfers between devices, per_device(): whole = lax.all_gather(columns, 'group', axis=1, tiled=True)  39 us
    psum x1, waiting for transfers between devices, per_device(): lax.psum(jnp.dot(difference, basis, precision=lax.Precision.HIGHEST), 'te...  22.1 us
    all_to_all x1, waiting for transfers between devices, per_device(): lax.all_to_all(stepped_half, 'shard', split_axis=2, concat_axis=1, tiled=...  21.9 us
    unnamed x12, local copies, waits for them, and re-layouts  21.6 us
    all_to_all x1, starting transfers between devices, per_device(): lax.all_to_all(part, 'shard', split_axis=1, concat_axis=2, tiled=True)  9.24 us
    all_to_all x1, starting transfers between devices, per_device(): lax.all_to_all(stepped_half, 'shard', split_axis=2, concat_axis=1, tiled=...  7.1 us
  transfers between devices with their start and end apart: 6, of which 5 were waited for; matrix products, arithmetic and copies ran while one was open for 10% of the time, Pallas kernels for 0%

commit v1 on v0

--- a/solution.py
+++ b/solution.py
@@ -26,7 +26,14 @@
     stepped = anchor - outer_rate * (delta + momentum_decay * moved)
     stepped_half = stepped.astype(jnp.bfloat16)
     columns = lax.all_to_all(stepped_half, "shard", split_axis=2, concat_axis=1, tiled=True)
-    whole = lax.all_gather(columns, "group", axis=1, tiled=True)
+
+    def extend_the_bars(payload):
+        w_next = jnp.stack([payload for _ in range(lax.psum(1, axis_name="group"))])
+        view_out = lax.all_to_all(w_next, axis_name="group", split_axis=0, concat_axis=0)
+        field_out = jnp.concatenate(view_out, axis=1)
+        return field_out
+
+    whole = extend_the_bars(columns)
     new_weights = whole.reshape(layers, width, block)
     local_embedding = group_embedding[0].astype(jnp.float32)
     emb_sum = lax.psum(local_embedding.astype(jnp.bfloat16), "group").astype(jnp.float32)

time: 261 us -> 285 us (1.092)
  blocking collectives: 0 us -> 57.8 us
  waiting for transfers between devices: 186 us -> 156 us
  starting transfers between devices: 16.7 us -> 10.3 us
  local copies, waits for them, and re-layouts: 23.8 us -> 27.1 us
    all_to_all x0 -> x1, blocking collectives: none -> 57.8 us  [per_device(): lax.all_to_all(part, 'shard', split_axis=1, concat_axis=2, tiled=True)]
    all_to_all x1, waiting for transfers between devices: 48.4 us -> 0.01 us  [extend_the_bars(): lax.all_to_all(w_next, axis_name='group', split_axis=0, concat_axis=0)]
    all_gather x1 -> x0, waiting for transfers between devices: 39 us -> none  [per_device(): whole = lax.all_gather(columns, 'group', axis=1, tiled=True)]
    psum x1, waiting for transfers between devices: 0.02 us -> 28.3 us  [per_device(): lax.psum(local_embedding.astype(jnp.bfloat16), 'group').astype(jnp.float32)]
    psum x1, waiting for transfers between devices: 22.1 us -> 48 us  [per_device(): lax.psum(jnp.dot(difference, basis, precision=lax.Precision.HIGHEST), 'te...]
    another operation x0 -> x3, local copies, waits for them, and re-layouts: none -> 7.15 us  [the longest x1 5.11 us: per_device(): new_weights = whole.reshape(layers, width, block)]
    unnamed x12 -> x13, local copies, waits for them, and re-layouts: 21.6 us -> 15.7 us
    all_to_all x1, starting transfers between devices: 9.24 us -> 3.62 us  [extend_the_bars(): lax.all_to_all(w_next, axis_name='group', split_axis=0, concat_axis=0)]
  transfers between devices with their start and end apart: 6 -> 5, of which waited for: 5 -> 4; matrix products, arithmetic and copies ran while one was open for 10% -> 7% of each run, Pallas kernels for 0% -> 0%
where the time goes in v1:
time: 285 us
  waiting for transfers between devices  156 us (55%)
  blocking collectives  57.8 us (20%)
  local copies, waits for them, and re-layouts  27.1 us (10%)
  between operations  13.8 us (5%)
  matrix products  11.7 us (4%)
  starting transfers between devices  10.3 us (4%)
  other arithmetic  7.91 us (3%)
    all_to_all x1, blocking collectives, per_device(): lax.all_to_all(part, 'shard', split_axis=1, concat_axis=2, tiled=True)  57.8 us
    reduce_scatter x1, waiting for transfers between devices, per_device(): lax.psum_scatter(local_weights.astype(jnp.float32).astype(jnp.bfloat16),...  53.3 us
    psum x1, waiting for transfers between devices, per_device(): lax.psum(jnp.dot(difference, basis, precision=lax.Precision.HIGHEST), 'te...  48 us
    psum x1, waiting for transfers between devices, per_device(): lax.psum(local_embedding.astype(jnp.bfloat16), 'group').astype(jnp.float32)  28.3 us
    all_to_all x1, waiting for transfers between devices, per_device(): lax.all_to_all(stepped_half, 'shard', split_axis=2, concat_axis=1, tiled=...  25.7 us
    unnamed x13, local copies, waits for them, and re-layouts  15.7 us
    dot_general x1, matrix products, per_device(): emb_delta = jnp.dot(coef, basis.T, precision=lax.Precision.HIGHEST)  6.94 us
    all_to_all x1, starting transfers between devices, per_device(): lax.all_to_all(stepped_half, 'shard', split_axis=2, concat_axis=1, tiled=...  6.37 us
  transfers between devices with their start and end apart: 5, of which 4 were waited for; matrix products, arithmetic and copies ran while one was open for 7% of the time, Pallas kernels for 0%

profile of v1, /device:TPU:1, one launch (start us, length us, event | category | flops | bytes accessed | tf_op | source)
XLA Modules:
  0.0 284.6 jit_solution(8560308159272836666)
XLA Ops:
  7.2 0.0 copy-start
  7.2 0.0 reduce-scatter.2.cloned.1.call-start
  7.2 6.8 %copy.30 = bf16[1,8,1024,136]{3,1,2,0:T(8,128)(2,1)} copy(bf16[1,8,1024,136]{2,3,1,0:T(8,128)(2,1)} %param.7) | data formatting | bytes 4456448 | tf_op args[0]
  14.0 0.0 reduce-scatter.2.cloned.1.call-update
  14.0 53.3 %reduce-scatter.2.cloned.1.call-done = bf16[8,256,136]{2,0,1:T(8,128)(2,1)} async-done(((bf16[8,1024,136]{2,0,1:T(8,128)(2,1)}), bf16[8,256,136]{2,0,1:T(8,128)(2,1)}) %reduce-scatter.2.cloned.1.call-update) | async-done | bytes 557072 | tf_op jit(solution)/shard_map/reduce_scatter | solution.py:16
  67.3 1.4 bitcast_convert_fusion
  68.7 57.8 %all_to_all.29 = f32[8,256,1,1,136]{4,0,3,2,1:T(8,128)S(1)} all-to-all(f32[8,256,1,1,136]{4,0,3,2,1:T(8,128)S(1)} %bitcast_convert_fusion), channel_id=1, replica_groups=mesh['group'=4,'shard'=16,'tensor'=4] {'shard'}, dimensions={1} | all-to-all | bytes 2228224 | tf_op jit(solution)/shard_map/all_to_all | solution.py:23
  126.5 0.7 copy_multiply_fusion.1
  127.2 0.8 copy-done.3
  128.0 0.6 copy-done.4
  128.7 5.8 %fusion.8 = (bf16[8,16,16,1,136]{4,1,2,0,3:T(8,128)(2,1)S(1)}, f32[8,16,16,1,136]{4,1,2,0,3:T(8,128)}, f32[8,16,16,1,136]{4,1,2,0,3:T(8,128)}) fusion(f32[8,16,16,1,136]{4,3,2,1,0:T(1,128)S(1)} %copy-done.3, f32[8,16,16,1,136]{4,1,2,0,3:T(8,128)S(1)} %bitcast.22, f32[8,16,16,1,136]{4,3,2,1,0:T(1,128)S(1)} %copy-done.4), kind=kLoop, calls=%fused_computation.15 | loop fusion | flops 2228224 | bytes 6127616 | tf_op jit(solution)/shard_map/convert_element_type | solution.py:27
  134.5 1.1 copy.35
  135.5 6.4 %all-to-all-start.1 = ((bf16[8,16,16,1,136]{4,1,0,3,2:T(8,128)(2,1)}), bf16[8,16,16,1,136]{4,1,0,3,2:T(8,128)(2,1)S(1)}, u32[]{:S(2)}, u32[]{:S(2)}) async-start(bf16[8,16,16,1,136]{4,1,0,3,2:T(8,128)(2,1)} %copy.35), calls=%async_computation.2 | async-start | bytes 2097152 | tf_op jit(solution)/shard_map/all_to_all | solution.py:28
  141.9 0.0 all-reduce.3.cloned.1.call-start
  142.0 0.7 all-reduce.3.cloned.1.call-update
  142.7 25.7 %all-to-all-done.1 = bf16[8,16,16,1,136]{4,1,0,3,2:T(8,128)(2,1)S(1)} async-done(((bf16[8,16,16,1,136]{4,1,0,3,2:T(8,128)(2,1)}), bf16[8,16,16,1,136]{4,1,0,3,2:T(8,128)(2,1)S(1)}, u32[]{:S(2)}, u32[]{:S(2)}) %all-to-all-start.1) | async-done | bytes 557088 | tf_op jit(solution)/shard_map/all_to_all | solution.py:28
  168.4 0.1 copy.36
  168.5 0.5 copy.37
  169.0 1.5 stack.10
  170.6 3.6 %all-to-all-start.2 = ((bf16[4,8,256,1,1,136]{2,5,1,4,3,0:T(8,128)(2,1)}), bf16[4,8,256,1,1,136]{2,5,1,4,3,0:T(8,128)(2,1)S(1)}, u32[]{:S(2)}, u32[]{:S(2)}) async-start(bf16[4,8,256,1,1,136]{2,5,1,4,3,0:T(8,128)(2,1)} %stack.10), calls=%async_computation.3 | async-start | bytes 4456448 | tf_op jit(solution)/shard_map/all_to_all | solution.py:32
  174.2 0.2 all-reduce.5.cloned.1.call-start
  174.4 28.3 %all-reduce.3.cloned.1.call-done = bf16[2000,256]{1,0:T(8,128)(2,1)} async-done(((bf16[2000,256]{1,0:T(8,128)(2,1)}), bf16[2000,256]{1,0:T(8,128)(2,1)}) %all-reduce.3.cloned.1.call-update) | async-done | bytes 1024016 | tf_op jit(solution)/shard_map/psum | solution.py:39
  202.7 0.0 copy-done
  202.7 4.8 %fusion.1 = f32[2000,64]{0,1:T(8,128)} fusion(f32[256,64]{0,1:T(8,128)S(1)} %copy-done, f32[2000,256]{1,0:T(8,128)} %param.11, bf16[2000,256]{1,0:T(8,128)(2,1)} %all-reduce.3.cloned.1.call-done), kind=kOutput, calls=%fused_computation.6 | convolution fusion | flops 394752000 | bytes 3649536 | tf_op jit(solution)/shard_map/dot_general | solution.py:41
  207.5 0.0 all-reduce.5.cloned.1.call-update
  207.5 48.0 %all-reduce.5.cloned.1.call-done = f32[2000,64]{0,1:T(8,128)} async-done(((f32[2000,64]{0,1:T(8,128)}), f32[2000,64]{0,1:T(8,128)}) %all-reduce.5.cloned.1.call-update) | async-done | bytes 512016 | tf_op jit(solution)/shard_map/psum | solution.py:41
  255.5 6.9 %fusion.7 = (bf16[2000,256]{1,0:T(8,128)(2,1)}, f32[2000,256]{1,0:T(8,128)}, f32[2000,256]{1,0:T(8,128)}) fusion(f32[2000,256]{1,0:T(8,128)} %param.11, f32[2000,256]{1,0:T(8,128)} %param.12, f32[2000,64]{0,1:T(8,128)} %all-reduce.5.cloned.1.call-done, f32[256,64]{0,1:T(8,128)S(1)} %copy-done), kind=kOutput, calls=%fused_computation.14 | convolution fusion | flops 396800000 | bytes 9793536 | tf_op jit(solution)/shard_map/dot_general | solution.py:42
  262.4 3.7 %copy.39 = f32[8,16,16,1,136]{4,3,2,1,0:T(1,128)} copy(f32[8,16,16,1,136]{4,1,2,0,3:T(8,128)S(1)} %copy-done.2) | data formatting | bytes 2228224
  266.1 3.7 %copy.40 = f32[8,16,16,1,136]{4,3,2,1,0:T(1,128)} copy(f32[8,16,16,1,136]{4,1,2,0,3:T(8,128)S(1)} %copy-done.1) | data formatting | bytes 2228224
  269.9 0.0 all-to-all-done.2
  269.9 3.1 %copy.38 = bf16[8,4,256,1,1,136]{2,1,5,0,4,3:T(4,128)(2,1)} copy(bf16[8,4,256,1,1,136]{2,5,0,4,3,1:T(8,128)(2,1)S(1)} %bitcast.21) | data formatting | bytes 4456448 | tf_op jit(solution)/shard_map/reshape | solution.py:33
  273.0 5.1 %reshape_reshape.3 = bf16[8,1024,136]{1,2,0:T(8,128)(2,1)} reshape(bf16[8,4,256,1,1,136]{2,1,5,0,4,3:T(4,128)(2,1)} %copy.38) | data formatting | bytes 4456448 | tf_op jit(solution)/shard_map/reshape;reshape | solution.py:37
  (6 shorter events, 0.0 us)
Async XLA Ops:
  7.2 195.5 %copy-start = (f32[256,64]{0,1:T(8,128)S(1)}, f32[256,64]{0,1:T(8,128)}, u32[]{:S(2)}) copy-start(f32[256,64]{0,1:T(8,128)} %param.13) | copy-start | bytes 196612
  7.2 60.1 %reduce-scatter.2.cloned.1.call-start = ((), (), s32[]{:S(2)}) async-start(), calls=%async_computation.4 | async-start | bytes 5242880 | tf_op jit(solution)/shard_map/reduce_scatter | solution.py:16
  126.4 1.6 copy-start.3
  126.5 2.2 copy-start.4
  135.5 32.9 %all-to-all-start.1 = ((bf16[8,16,16,1,136]{4,1,0,3,2:T(8,128)(2,1)}), bf16[8,16,16,1,136]{4,1,0,3,2:T(8,128)(2,1)S(1)}, u32[]{:S(2)}, u32[]{:S(2)}) async-start(bf16[8,16,16,1,136]{4,1,0,3,2:T(8,128)(2,1)} %copy.35), calls=%async_computation.2 | async-start | bytes 2097152 | tf_op jit(solution)/shard_map/all_to_all | solution.py:28
  141.9 60.8 %all-reduce.3.cloned.1.call-start = ((), (), s32[]{:S(2)}) async-start(), calls=%async_computation.5 | async-start | bytes 2048000 | tf_op jit(solution)/shard_map/psum | solution.py:39
  170.6 99.3 %all-to-all-start.2 = ((bf16[4,8,256,1,1,136]{2,5,1,4,3,0:T(8,128)(2,1)}), bf16[4,8,256,1,1,136]{2,5,1,4,3,0:T(8,128)(2,1)S(1)}, u32[]{:S(2)}, u32[]{:S(2)}) async-start(bf16[4,8,256,1,1,136]{2,5,1,4,3,0:T(8,128)(2,1)} %stack.10), calls=%async_computation.3 | async-start | bytes 4456448 | tf_op jit(solution)/shard_map/all_to_all | solution.py:32
  174.2 81.3 %all-reduce.5.cloned.1.call-start = ((), (), s32[]{:S(2)}) async-start(), calls=%async_computation.6 | async-start | bytes 1048576 | tf_op jit(solution)/shard_map/psum | solution.py:41
  255.5 6.9 %copy-start.2 = (f32[8,16,16,1,136]{4,1,2,0,3:T(8,128)S(1)}, f32[8,16,16,1,136]{4,1,2,0,3:T(8,128)}, u32[]{:S(2)}) copy-start(f32[8,16,16,1,136]{4,1,2,0,3:T(8,128)} %get-tuple-element.28) | copy-start | bytes 3342340
  262.4 3.7 %copy-start.1 = (f32[8,16,16,1,136]{4,1,2,0,3:T(8,128)S(1)}, f32[8,16,16,1,136]{4,1,2,0,3:T(8,128)}, u32[]{:S(2)}) copy-start(f32[8,16,16,1,136]{4,1,2,0,3:T(8,128)} %get-tuple-element.29) | copy-start | bytes 3342340
Sparse Core Ops, SparseCore 0:
  14.1 53.1 reduce-scatter.1
  145.1 57.5 all-reduce.2
  207.6 47.7 all-reduce.4
